TPU v7x, 512 devices: a whole 4x4x16 slice. The times are simulated.
512 devices in a mesh: box: 8 (over z_lo, core), panel: 64 (over y, x, z_hi).
Axes of the slice: x: 4, y: 4, z: 16 (z_hi: 4, z_lo: 4; z = z_hi * 4 + z_lo), core: 2. Of those that a mesh axis runs over, the one named last changes fastest.
Arguments:
- exterior_rows: float32 [8, 2048, 2, 128], P('box'), may hold values from -6 to 6
- exterior_block: float32 [8, 6144, 2, 128], P('box', 'panel'), may hold values from -6 to 6
- shared_block: float32 [8, 2048, 2, 2048], P('box', 'panel'), may hold values from -0.9 to 0.9
- crossing_block: float32 [8, 6144, 2, 2048], P('box', 'panel'), may hold values from -0.125 to 0.125
Outputs:
- merged_map: float32 [8, 2, 6144, 2, 128], P('box', None, 'panel')
All inputs are finite; a program needn't handle non-finite values.
Results may differ from a plain program's by a relative error of at most 0.0001.
Values sent between devices are 32-bit elements; how exact they have to be, the bound alone decides.
No kernel may reach another device: no remote copies, remote signals or barrier semaphores. Data moves between devices by JAX's collectives and lax.ppermute only.
A program may use at most 64 MiB of HBM per device.

v0:
```python
import jax
import jax.numpy as jnp
from jax import lax
from jax.sharding import PartitionSpec as P

ITERS = 3


def swapped(shard, axis, bit):
    return lax.ppermute(shard, axis, [(i, i ^ 1 << bit) for i in range(lax.axis_size(axis))])


def complex_product(left_factor, operand):
    highest = lax.Precision.HIGHEST
    real_part = jnp.dot(
        left_factor[:, 0], operand[:, 0], precision=highest, preferred_element_type=jnp.float32
    ) - jnp.dot(
        left_factor[:, 1], operand[:, 1], precision=highest, preferred_element_type=jnp.float32
    )
    imag_part = jnp.dot(
        left_factor[:, 0], operand[:, 1], precision=highest, preferred_element_type=jnp.float32
    ) + jnp.dot(
        left_factor[:, 1], operand[:, 0], precision=highest, preferred_element_type=jnp.float32
    )
    return jnp.stack([real_part, imag_part], axis=1)


def slice_product(matrix, gathered_piece):
    return complex_product(matrix, gathered_piece)


def local(exterior_rows, exterior_block, shared_block, crossing_block):
    start_rows = exterior_rows[0]
    own_exterior = exterior_block[0]
    own_shared = shared_block[0]
    own_crossing = crossing_block[0]
    width_panel = own_shared.shape[0]
    panel_index = lax.axis_index("panel")
    own_rows = lax.dynamic_slice_in_dim(start_rows, panel_index * width_panel, width_panel, 0)
    other_form, other_crossing = swapped((own_shared, own_crossing), "box", 0)

    def through_own(gathered_piece):
        return slice_product(own_shared, gathered_piece)

    def own_step(image_now):
        return own_rows + through_own(lax.all_gather(image_now, "panel", axis=0, tiled=True))

    image_panel = complex_product(other_form, start_rows)
    rows_panel = own_step(image_panel)
    for iteration in range(1, ITERS):
        image_panel = slice_product(
            other_form, lax.all_gather(rows_panel, "panel", axis=0, tiled=True)
        )
        rows_panel = own_step(image_panel)
    gathered_piece = lax.all_gather(rows_panel, "panel", axis=0, tiled=True)
    image_final = slice_product(other_form, gathered_piece)
    other_terms = slice_product(other_crossing, gathered_piece)
    own_terms = slice_product(
        own_crossing, lax.all_gather(image_final, "panel", axis=0, tiled=True)
    )
    merged = jnp.stack([own_exterior + own_terms, -other_terms], axis=0)
    return merged[None]


def solution(mesh):
    return jax.shard_map(
        local,
        mesh=mesh,
        in_specs=(
            P("box", None, None, None),
            P("box", "panel", None, None),
            P("box", "panel", None, None),
            P("box", "panel", None, None),
        ),
        out_specs=P("box", None, "panel", None, None),
        check_vma=False,
    )
```

profile of v0, /device:TPU:4, one launch (start us, length us, event | category | flops | bytes accessed | tf_op | source)
XLA Modules:
  0.0 853.4 jit_solution(4631152785487353609)
XLA Ops:
  6.5 1.9 collective-permute-start
  8.5 4.0 fusion.108
  12.5 0.4 fusion.112
  12.9 0.7 fusion.68
  13.6 0.7 fusion.70
  14.3 0.7 fusion.16
  15.1 0.7 fusion.17
  15.8 0.6 pad_maximum_fusion
  16.4 0.0 all-gather.10.cloned.1.call-start
  16.5 0.8 constant_dynamic-slice_fusion
  17.2 0.4 fusion.111
  17.6 119.2 %all-gather.8.cloned.1.call-done = f32[2048,2,128]{2,0,1:T(8,128)} async-done(((f32[32,2,128]{2,0,1:T(8,128)}), f32[2048,2,128]{2,0,1:T(8,128)}) %all-gather.8.cloned.1.call-update) | async-done | bytes 2097168 | tf_op jit(solution)/shard_map/all_gather | solution.py:46
  136.8 2.1 fusion.19
  138.9 2.0 fusion.18
  140.9 0.8 fusion.14
  141.7 0.8 fusion.15
  142.4 0.6 maximum_add_fusion.1
  143.1 0.0 all-gather.12.cloned.1.call-start
  143.1 110.5 %all-gather.10.cloned.1.call-done = f32[2048,2,128]{2,0,1:T(8,128)} async-done(((f32[32,2,128]{2,0,1:T(8,128)}), f32[2048,2,128]{2,0,1:T(8,128)}) %all-gather.10.cloned.1.call-update) | async-done | bytes 2097168 | tf_op jit(solution)/shard_map/all_gather | solution.py:52
  253.6 2.1 fusion.20
  255.8 2.0 fusion.21
  257.7 0.8 fusion.12
  258.5 0.8 fusion.13
  259.3 0.6 pad_maximum_fusion.1
  259.9 0.2 all-gather.14.cloned.1.call-start
  260.1 110.3 %all-gather.12.cloned.1.call-done = f32[2048,2,128]{2,0,1:T(8,128)} async-done(((f32[32,2,128]{2,0,1:T(8,128)}), f32[2048,2,128]{2,0,1:T(8,128)}) %all-gather.12.cloned.1.call-update) | async-done | bytes 2097168 | tf_op jit(solution)/shard_map/all_gather | solution.py:46
  370.5 2.1 fusion.23
  372.6 2.0 fusion.22
  374.6 0.8 fusion.10
  375.4 0.8 fusion.11
  376.1 0.6 maximum_add_fusion.2
  376.8 0.0 all-gather.16.cloned.1.call-start
  376.8 110.5 %all-gather.14.cloned.1.call-done = f32[2048,2,128]{2,0,1:T(8,128)} async-done(((f32[32,2,128]{2,0,1:T(8,128)}), f32[2048,2,128]{2,0,1:T(8,128)}) %all-gather.14.cloned.1.call-update) | async-done | bytes 2097168 | tf_op jit(solution)/shard_map/all_gather | solution.py:52
  487.3 2.1 fusion.24
  489.5 2.0 fusion.25
  491.4 0.8 fusion.8
  492.2 0.8 fusion.9
  493.0 0.6 pad_maximum_fusion.2
  493.6 0.0 all-gather.18.cloned.1.call-start
  493.7 110.5 %all-gather.16.cloned.1.call-done = f32[2048,2,128]{2,0,1:T(8,128)} async-done(((f32[32,2,128]{2,0,1:T(8,128)}), f32[2048,2,128]{2,0,1:T(8,128)}) %all-gather.16.cloned.1.call-update) | async-done | bytes 2097168 | tf_op jit(solution)/shard_map/all_gather | solution.py:46
  604.2 2.1 fusion.27
  606.3 2.0 fusion.26
  608.3 0.8 fusion.6
  609.1 0.8 fusion.7
  609.8 0.6 maximum_add_fusion.3
  610.5 110.5 %all-gather.18.cloned.1.call-done = f32[2048,2,128]{2,0,1:T(8,128)} async-done(((f32[32,2,128]{2,0,1:T(8,128)}), f32[2048,2,128]{2,0,1:T(8,128)}) %all-gather.18.cloned.1.call-update) | async-done | bytes 2097168 | tf_op jit(solution)/shard_map/all_gather | solution.py:55
  721.0 2.1 fusion.31
  723.2 2.0 fusion.33
  725.1 0.8 fusion.4
  725.9 0.8 fusion.5
  726.6 0.6 pad_maximum_fusion.3
  727.3 2.1 collective-permute-start.1
  729.4 4.5 fusion.109
  733.9 1.2 fusion.110
  735.1 1.3 fusion.30
  736.4 1.3 fusion
  737.7 1.3 fusion.32
  738.9 1.3 fusion.1
  740.2 97.6 %all-gather.20.cloned.1.call-done = f32[2048,2,128]{2,0,1:T(8,128)} async-done(((f32[32,2,128]{2,0,1:T(8,128)}), f32[2048,2,128]{2,0,1:T(8,128)}) %all-gather.20.cloned.1.call-update) | async-done | bytes 2097168 | tf_op jit(solution)/shard_map/all_gather | solution.py:59
  837.9 2.6 fusion.29
  840.4 2.4 fusion.28
  842.9 1.2 fusion.2
  844.1 1.2 fusion.3
  845.3 0.8 copy.7
  (34 shorter events, 0.2 us)
Async XLA Ops:
  6.5 130.3 %all-gather.8.cloned.1.call-start = ((), (), s32[]{:S(2)}) async-start(), calls=%async_computation | async-start | bytes 2129920 | tf_op jit(solution)/shard_map/all_gather | solution.py:46
  6.5 6.0 collective-permute-start
  13.6 3.6 copy-start.8
  16.4 237.2 %all-gather.10.cloned.1.call-start = ((), (), s32[]{:S(2)}) async-start(), calls=%async_computation.1 | async-start | bytes 2129920 | tf_op jit(solution)/shard_map/all_gather | solution.py:52
  136.8 4.1 copy-start.2
  143.1 227.4 %all-gather.12.cloned.1.call-start = ((), (), s32[]{:S(2)}) async-start(), calls=%async_computation.2 | async-start | bytes 2129920 | tf_op jit(solution)/shard_map/all_gather | solution.py:46
  253.6 4.1 copy-start.4
  259.9 227.4 %all-gather.14.cloned.1.call-start = ((), (), s32[]{:S(2)}) async-start(), calls=%async_computation.3 | async-start | bytes 2129920 | tf_op jit(solution)/shard_map/all_gather | solution.py:52
  370.5 4.1 copy-start.5
  376.8 227.4 %all-gather.16.cloned.1.call-start = ((), (), s32[]{:S(2)}) async-start(), calls=%async_computation.4 | async-start | bytes 2129920 | tf_op jit(solution)/shard_map/all_gather | solution.py:46
  487.3 4.1 copy-start.6
  493.6 227.4 %all-gather.18.cloned.1.call-start = ((), (), s32[]{:S(2)}) async-start(), calls=%async_computation.5 | async-start | bytes 2129920 | tf_op jit(solution)/shard_map/all_gather | solution.py:55
  604.2 4.1 copy-start.3
  610.5 227.4 %all-gather.20.cloned.1.call-start = ((), (), s32[]{:S(2)}) async-start(), calls=%async_computation.6 | async-start | bytes 2129920 | tf_op jit(solution)/shard_map/all_gather | solution.py:59
  721.0 4.1 copy-start
  727.3 6.6 collective-permute-start.1
  740.2 102.7 %copy-start.7 = (f32[96,1,2048]{2,1,0:T(1,128)S(1)}, f32[96,1,2048]{2,1,0:T(1,128)}, u32[]{:S(2)}) copy-start(f32[96,1,2048]{2,1,0:T(1,128)} %get-tuple-element.7) | copy-start | bytes 2359300
  837.9 5.0 copy-start.1
  842.8 2.4 copy-start.9
Sparse Core Ops, SparseCore 0:
  16.5 120.2 all-gather.7
  143.2 110.4 all-gather.9
  260.0 110.4 all-gather.11
  376.9 110.4 all-gather.13
  493.7 110.4 all-gather.15
  610.6 110.4 all-gather.17
  727.4 110.4 all-gather.19
where the time goes:
time: 862 us; the launch traced here: 853 us
  waiting for transfers between devices  769 us (89%)
  matrix products  48.9 us (6%)
  between operations  14.1 us (2%)
  local copies, waits for them, and re-layouts  12.2 us (1%)
    all_gather x3, waiting for transfers between devices, own_step(): lax.all_gather(image_now, 'panel', axis=0, tiled=True)  340 us
    all_gather x2, waiting for transfers between devices, local(): lax.all_gather(rows_panel, 'panel', axis=0, tiled=True)  221 us
    all_gather x1, waiting for transfers between devices, local(): gathered_piece = lax.all_gather(rows_panel, 'panel', axis=0, tiled=True)  111 us
    all_gather x1, waiting for transfers between devices, local(): lax.all_gather(image_final, 'panel', axis=0, tiled=True)  97.6 us
  transfers between devices with their start and end apart: 9, of which 7 were waited for; matrix products, arithmetic and copies ran while one was open for 2% of the time, Pallas kernels for 0%

commit v1 on v0

--- a/solution.py
+++ b/solution.py
@@ -43,7 +43,12 @@
         return slice_product(own_shared, gathered_piece)
 
     def own_step(image_now):
-        return own_rows + through_own(lax.all_gather(image_now, "panel", axis=0, tiled=True))
+        return own_rows + through_own(
+            jnp.concatenate(
+                lax.all_to_all(jnp.stack([image_now] * lax.axis_size("panel")), "panel", 0, 0),
+                axis=0,
+            )
+        )
 
     image_panel = complex_product(other_form, start_rows)
     rows_panel = own_step(image_panel)

time: 862 us -> 855 us (level)
  waiting for transfers between devices: 769 us -> 520 us
  blocking collectives: 0 us -> 219 us
  starting transfers between devices: 4.47 us -> 26.4 us
  local copies, waits for them, and re-layouts: 12.2 us -> 23.9 us
    all_gather x3 -> x0, waiting for transfers between devices: 340 us -> none  [own_step(): lax.all_gather(image_now, 'panel', axis=0, tiled=True)]
    all_to_all x0 -> x2, blocking collectives: none -> 219 us  [own_step(): lax.all_to_all(jnp.stack([image_now] * lax.axis_size('panel')), 'panel',...]
    all_to_all x0 -> x1, waiting for transfers between devices: none -> 96 us  [own_step(): lax.all_to_all(jnp.stack([image_now] * lax.axis_size('panel')), 'panel',...]
    all_to_all x0 -> x1, starting transfers between devices: none -> 21.6 us  [own_step(): lax.all_to_all(jnp.stack([image_now] * lax.axis_size('panel')), 'panel',...]
  transfers between devices with their start and end apart: 9 -> 7, of which waited for: 7 -> 5; matrix products, arithmetic and copies ran while one was open for 2% -> 2% of each run, Pallas kernels for 0% -> 0%
where the time goes in v1:
time: 855 us; the launch traced here: 847 us
  waiting for transfers between devices  520 us (61%)
  blocking collectives  219 us (26%)
  matrix products  41 us (5%)
  starting transfers between devices  26.4 us (3%)
  local copies, waits for them, and re-layouts  23.9 us (3%)
  between operations  13.8 us (2%)
    all_to_all x2, blocking collectives, own_step(): lax.all_to_all(jnp.stack([image_now] * lax.axis_size('panel')), 'panel',...  219 us
    all_gather x2, waiting for transfers between devices, local(): lax.all_gather(rows_panel, 'panel', axis=0, tiled=True)  218 us
    all_gather x1, waiting for transfers between devices, local(): gathered_piece = lax.all_gather(rows_panel, 'panel', axis=0, tiled=True)  108 us
    all_gather x1, waiting for transfers between devices, local(): lax.all_gather(image_final, 'panel', axis=0, tiled=True)  97.6 us
    all_to_all x1, waiting for transfers between devices, own_step(): lax.all_to_all(jnp.stack([image_now] * lax.axis_size('panel')), 'panel',...  96 us
    all_to_all x1, starting transfers between devices, own_step(): lax.all_to_all(jnp.stack([image_now] * lax.axis_size('panel')), 'panel',...  21.6 us
  transfers between devices with their start and end apart: 7, of which 5 were waited for; matrix products, arithmetic and copies ran while one was open for 2% of the time, Pallas kernels for 0%

profile of v1, /device:TPU:4, one launch (start us, length us, event | category | flops | bytes accessed | tf_op | source)
XLA Modules:
  0.0 847.0 jit_solution(15212891502444263396)
XLA Ops:
  6.5 1.9 collective-permute-start
  8.5 4.0 fusion.111
  12.5 0.4 fusion.115
  12.9 0.7 fusion.68
  13.6 0.7 fusion.70
  14.3 0.7 fusion.16
  15.0 0.7 fusion.17
  15.8 2.3 stack.65
  18.1 21.6 %all-to-all-start = ((f32[64,32,2,128]{3,2,1,0:T(2,128)}), f32[64,32,2,128]{3,2,1,0:T(2,128)}, u32[]{:S(2)}, u32[]{:S(2)}) async-start(f32[64,32,2,128]{3,2,1,0:T(2,128)} %stack.65), calls=%async_computation | async-start | bytes 4194304 | tf_op jit(solution)/shard_map/all_to_all | solution.py:48
  39.7 0.8 constant_dynamic-slice_fusion
  40.5 0.4 fusion.114
  40.9 96.0 %all-to-all-done = f32[64,32,2,128]{3,2,1,0:T(2,128)} async-done(((f32[64,32,2,128]{3,2,1,0:T(2,128)}), f32[64,32,2,128]{3,2,1,0:T(2,128)}, u32[]{:S(2)}, u32[]{:S(2)}) %all-to-all-start) | async-done | bytes 2097184 | tf_op jit(solution)/shard_map/all_to_all | solution.py:48
  136.9 4.0 fusion.110
  140.9 0.8 fusion.58
  141.7 0.8 fusion.60
  142.4 0.8 fusion.14
  143.2 0.8 fusion.15
  143.9 0.6 maximum_add_fusion.1
  144.6 0.5 all-gather.7.cloned.1.call-start
  145.1 110.1 %all-gather.5.cloned.1.call-done = f32[2048,2,128]{2,0,1:T(8,128)} async-done(((f32[32,2,128]{2,0,1:T(8,128)}), f32[2048,2,128]{2,0,1:T(8,128)}) %all-gather.5.cloned.1.call-update) | async-done | bytes 2097168 | tf_op jit(solution)/shard_map/all_gather | solution.py:57
  255.2 2.1 fusion.18
  257.3 2.0 fusion.19
  259.3 0.8 fusion.12
  260.0 0.8 fusion.13
  260.9 1.0 stack.72
  261.9 109.5 %all_to_all.15 = f32[64,32,2,128]{3,2,1,0:T(2,128)S(1)} all-to-all(f32[64,32,2,128]{3,2,1,0:T(2,128)S(1)} %stack.72), channel_id=1, replica_groups=mesh['box'=8,'panel'=64] {'panel'}, dimensions={0} | all-to-all | bytes 4194304 | tf_op jit(solution)/shard_map/all_to_all | solution.py:48
  371.3 1.6 fusion.109
  373.0 0.8 fusion.54
  373.8 0.8 fusion.56
  374.5 0.8 fusion.10
  375.3 0.8 fusion.11
  376.0 0.6 maximum_add_fusion.2
  376.9 108.2 %all-gather.7.cloned.1.call-done = f32[2048,2,128]{2,0,1:T(8,128)} async-done(((f32[32,2,128]{2,0,1:T(8,128)}), f32[2048,2,128]{2,0,1:T(8,128)}) %all-gather.7.cloned.1.call-update) | async-done | bytes 2097168 | tf_op jit(solution)/shard_map/all_gather | solution.py:57
  485.1 2.1 fusion.20
  487.2 2.0 fusion.21
  489.2 0.8 fusion.8
  489.9 0.8 fusion.9
  490.8 1.0 stack.79
  491.8 109.5 %all_to_all.16 = f32[64,32,2,128]{3,2,1,0:T(2,128)S(1)} all-to-all(f32[64,32,2,128]{3,2,1,0:T(2,128)S(1)} %stack.79), channel_id=1, replica_groups=mesh['box'=8,'panel'=64] {'panel'}, dimensions={0} | all-to-all | bytes 4194304 | tf_op jit(solution)/shard_map/all_to_all | solution.py:48
  601.3 1.6 fusion.108
  602.9 0.8 fusion.50
  603.7 0.8 fusion.52
  604.4 0.8 fusion.6
  605.2 0.8 fusion.7
  605.9 0.6 maximum_add_fusion.3
  606.6 108.4 %all-gather.9.cloned.1.call-done = f32[2048,2,128]{2,0,1:T(8,128)} async-done(((f32[32,2,128]{2,0,1:T(8,128)}), f32[2048,2,128]{2,0,1:T(8,128)}) %all-gather.9.cloned.1.call-update) | async-done | bytes 2097168 | tf_op jit(solution)/shard_map/all_gather | solution.py:60
  715.0 2.1 fusion.25
  717.1 2.0 fusion.27
  719.1 0.8 fusion.4
  719.8 0.8 fusion.5
  720.6 0.6 pad_maximum_fusion.3
  721.2 2.1 collective-permute-start.1
  723.4 4.5 fusion.112
  727.9 1.2 fusion.113
  729.1 1.3 fusion.24
  730.3 1.3 fusion
  731.6 1.3 fusion.26
  732.9 1.3 fusion.1
  734.2 97.6 %all-gather.11.cloned.1.call-done = f32[2048,2,128]{2,0,1:T(8,128)} async-done(((f32[32,2,128]{2,0,1:T(8,128)}), f32[2048,2,128]{2,0,1:T(8,128)}) %all-gather.11.cloned.1.call-update) | async-done | bytes 2097168 | tf_op jit(solution)/shard_map/all_gather | solution.py:64
  831.8 2.6 fusion.23
  834.4 2.4 fusion.22
  836.8 1.2 fusion.2
  838.0 1.2 fusion.3
  839.2 0.8 copy.10
  (32 shorter events, 0.5 us)
Async XLA Ops:
  6.5 6.0 collective-permute-start
  18.1 22.4 %copy-start.5 = (f32[1,32,2,2048]{3,2,1,0:T(2,128)S(1)}, f32[1,32,2,2048]{3,2,1,0:T(2,128)}, u32[]{:S(2)}) copy-start(f32[1,32,2,2048]{3,2,1,0:T(2,128)} %param.6) | copy-start | bytes 1572868
  18.1 118.8 %all-to-all-start = ((f32[64,32,2,128]{3,2,1,0:T(2,128)}), f32[64,32,2,128]{3,2,1,0:T(2,128)}, u32[]{:S(2)}, u32[]{:S(2)}) async-start(f32[64,32,2,128]{3,2,1,0:T(2,128)} %stack.65), calls=%async_computation | async-start | bytes 4194304 | tf_op jit(solution)/shard_map/all_to_all | solution.py:48
  39.7 215.5 %all-gather.5.cloned.1.call-start = ((), (), s32[]{:S(2)}) async-start(), calls=%async_computation.3 | async-start | bytes 2129920 | tf_op jit(solution)/shard_map/all_gather | solution.py:57
  144.6 340.5 %all-gather.7.cloned.1.call-start = ((), (), s32[]{:S(2)}) async-start(), calls=%async_computation.4 | async-start | bytes 2129920 | tf_op jit(solution)/shard_map/all_gather | solution.py:57
  255.2 4.1 copy-start.2
  376.7 338.3 %all-gather.9.cloned.1.call-start = ((), (), s32[]{:S(2)}) async-start(), calls=%async_computation.5 | async-start | bytes 2129920 | tf_op jit(solution)/shard_map/all_gather | solution.py:60
  485.1 4.1 copy-start.3
  606.6 225.2 %all-gather.11.cloned.1.call-start = ((), (), s32[]{:S(2)}) async-start(), calls=%async_computation.6 | async-start | bytes 2129920 | tf_op jit(solution)/shard_map/all_gather | solution.py:64
  715.0 4.1 copy-start
  721.2 6.6 collective-permute-start.1
  734.1 102.7 %copy-start.4 = (f32[96,1,2048]{2,1,0:T(1,128)S(1)}, f32[96,1,2048]{2,1,0:T(1,128)}, u32[]{:S(2)}) copy-start(f32[96,1,2048]{2,1,0:T(1,128)} %get-tuple-element.13) | copy-start | bytes 2359300
  831.8 5.0 copy-start.1
  836.8 2.4 copy-start.6
Sparse Core Ops, SparseCore 0:
  144.7 110.4 all-gather.4
  376.8 108.2 all-gather.6
  606.7 108.2 all-gather.8
  721.4 110.4 all-gather.10
